TPU v7x, 32 devices: a whole 2x2x4 slice. The times are simulated.
32 devices in a mesh: region: 8 (over y, x, core), dom: 4 (over z).
Axes of the slice: x: 2, y: 2, z: 4, core: 2. Of those that a mesh axis runs over, the one named last changes fastest.
Arguments:
- feats: bfloat16 [16384, 512], P(('region', 'dom')), may hold values from -6 to 6
- hub_feats: bfloat16 [64, 512], P('region'), may hold values from -6 to 6
- hub_ids: int32 [16384, 4], P(('region', 'dom')), may hold values from 0 to 63
- tile_src: int32 [512], P(('region', 'dom')), may hold values from 0 to 4
- tile_mask: int32 [512, 128, 128], P(('region', 'dom')), may hold values 0 or 1
- w_stack: bfloat16 [1024, 512], replicated, may hold values from -0.1875 to 0.1875
- cotangent: bfloat16 [16384, 512], P(('region', 'dom')), may hold values from -6 to 6
Outputs:
- activ: bfloat16 [16384, 512], P(('region', 'dom'))
- weight_grad: float32 [1024, 512], P('dom')
- hub_grad: float32 [64, 512], P('region')
Inputs may be any that keep to these rules, and one draw needn't show every extreme that they name: tile_src names a block of the part's window: 0 is the block taken from the previous part, 1 to 4 are the part's own blocks. `hub_ids`: hub ids index rows of hub_feats.
All inputs are finite; a program needn't handle non-finite values. No bound on the sum of `tile_mask` on one device may be relied on, other than what follows from the above.
Results may differ from a plain program's by a relative error of at most 0.0051.
Values may be sent and summed in bfloat16 or wider, within the bound.
No kernel may reach another device: no remote copies, remote signals or barrier semaphores. Data moves between devices by JAX's collectives and lax.ppermute only.
A program may use at most 64 MiB of HBM per device.

v0:
```python
import jax
import jax.numpy as jnp
from jax import lax
from jax.sharding import PartitionSpec as P


def shifted(value, axis, steps):
    count = lax.axis_size(axis)
    initial, last = (max(0, -steps), min(count, count - steps))
    return lax.ppermute(value, axis, [(source, source + steps) for source in range(initial, last)])


def on_device(feats, hub_feats, hub_ids, tile_src, tile_mask, w_stack, cotangent):
    rows, width = feats.shape
    tile = tile_mask.shape[1]
    nblk = rows // tile
    per_block = tile_src.shape[0] // nblk
    hub_count = hub_ids.shape[1]
    owned = hub_feats.shape[0]
    total_hubs = owned * lax.axis_size("region")
    prev = shifted(feats[rows - tile :], "dom", 1)
    window = jnp.concatenate([prev, feats], axis=0).reshape(nblk + 1, tile, width)
    picked = jnp.take(window, tile_src, axis=0)
    mask_b = tile_mask.astype(jnp.bfloat16)
    prod = jnp.einsum("tij,tjd->tid", mask_b, picked, preferred_element_type=jnp.float32)
    nsum = prod.reshape(nblk, per_block, tile, width).sum(axis=1).reshape(rows, width)
    cnt = tile_mask.reshape(nblk, per_block, tile, tile).sum(axis=(1, 3)).reshape(rows)
    deg = 1.0 + cnt.astype(jnp.float32) + jnp.float32(hub_count)
    hub_cols = lax.broadcasted_iota(jnp.int32, (rows, total_hubs), 1)
    counts = jnp.zeros((rows, total_hubs), jnp.float32)
    for slot in range(hub_count):
        counts = counts + (hub_ids[:, slot : slot + 1] == hub_cols).astype(jnp.float32)
    counts = counts.astype(jnp.bfloat16)
    block = counts
    hsum = jnp.dot(
        block,
        lax.all_gather(hub_feats, "region", axis=0, tiled=True),
        preferred_element_type=jnp.float32,
    )
    agg = ((feats.astype(jnp.float32) + nsum + hsum) / deg[:, None]).astype(jnp.bfloat16)
    inputs = jnp.concatenate([feats, agg], axis=1)
    z = jnp.dot(inputs, w_stack, preferred_element_type=jnp.float32)
    sig = jax.nn.sigmoid(z)
    activ = (z * sig).astype(jnp.bfloat16)
    dz = (cotangent.astype(jnp.float32) * sig * (1.0 + z * (1.0 - sig))).astype(jnp.bfloat16)
    partial_w = lax.psum_scatter(
        lax.dot_general(inputs, dz, (((0,), (0,)), ((), ())), preferred_element_type=jnp.float32),
        "dom",
        scatter_dimension=0,
        tiled=True,
    )
    weight_grad = lax.psum(partial_w, "region")
    dagg = lax.dot_general(
        dz, w_stack[width:], (((1,), (1,)), ((), ())), preferred_element_type=jnp.float32
    )
    sgrad = (dagg / deg[:, None]).astype(jnp.bfloat16)
    block = counts
    region_sum = lax.psum_scatter(
        lax.dot_general(block, sgrad, (((0,), (0,)), ((), ())), preferred_element_type=jnp.float32),
        "region",
        scatter_dimension=0,
        tiled=True,
    )
    hub_grad = lax.psum(region_sum, "dom")
    return (activ, weight_grad, hub_grad)


def solution(mesh):
    placed = (
        P(("region", "dom"), None),
        P("region", None),
        P(("region", "dom"), None),
        P(("region", "dom")),
        P(("region", "dom"), None, None),
        P(),
        P(("region", "dom"), None),
    )
    return jax.shard_map(
        on_device,
        mesh=mesh,
        in_specs=placed,
        out_specs=(P(("region", "dom"), None), P("dom", None), P("region", None)),
        check_vma=False,
    )
```

profile of v0, /device:TPU:0, one launch (start us, length us, event | category | flops | bytes accessed | tf_op | source)
XLA Modules:
  0.0 183.3 jit_solution(3585333480241991576)
XLA Ops:
  7.2 0.0 reduce-scatter.3.cloned.1.call-start
  7.2 1.0 slice.18
  8.2 5.0 %collective-permute-start = (bf16[128,512]{1,0:T(8,128)(2,1)S(1)}, bf16[128,512]{1,0:T(8,128)(2,1)S(1)}, u32[]{:S(2)}, u32[]{:S(2)}) collective-permute-start(bf16[128,512]{1,0:T(8,128)(2,1)S(1)} %slice.18), channel_id=1, source_target_pairs={{0,1},{1,2},{2,3},{4,5},{5,6},{6,7},{8,9},{9,10},{10,11},{12,13},{... | collective-permute-start | bytes 393224 | tf_op jit(solution)/shard_map/ppermute | solution.py:10
  13.2 1.6 reduce_sum.26
  14.8 0.9 fusion.19
  15.6 0.7 compare_select_fusion
  16.3 0.7 compare_and_fusion
  17.0 1.3 copy.23
  18.2 9.3 %all_gather.3 = bf16[64,512]{1,0:T(8,128)(2,1)S(1)} all-gather(bf16[8,512]{1,0:T(8,128)(2,1)S(1)} %copy-done.2), channel_id=1, replica_groups=mesh['region'=8,'dom'=4] {'region'}, dimensions={0}, use_global_device_ids=true | all-gather | bytes 73728 | tf_op jit(solution)/shard_map/all_gather | solution.py:37
  27.6 2.0 %gather_fusion = bf16[16,128,512]{2,1,0:T(8,128)(2,1)} fusion(bf16[5,128,512]{2,1,0:T(8,128)(2,1)S(1)} %bitcast.23, s32[1024]{0:T(1024)S(1)} %pad_clamp_fusion), kind=kCustom, calls=%fused_computation | custom fusion | bytes 4194368 | tf_op jit(solution)/shard_map/jit(_take)/gather | solution.py:23
  29.6 2.6 %bitcast_reduce_fusion = f32[4,128,512]{1,2,0:T(8,128)S(1)} fusion(bf16[16,128,512]{2,1,0:T(8,128)(2,1)} %gather_fusion, pred[16]{0:T(512)(128)(4,1)S(1)} %compare_and_fusion, s32[16,128,128]{2,1,0:T(8,128)S(1)} %copy-done.1), kind=kOutput, calls=%fused_computation.1 | convolution fusion | flops 270532608 | bytes 4194320 | tf_op jit(solution)/shard_map/tij,tjd->tid/dot_general | solution.py:25
  32.2 1.0 fusion.6
  33.2 0.2 copy-done.3
  33.4 0.1 copy-done.4
  33.6 1.9 %multiply_convert_fusion = (bf16[512,512]{1,0:T(8,128)(2,1)S(1)}, bf16[512,512]{1,0:T(8,128)(2,1)}) fusion(bf16[512,512]{1,0:T(8,128)(2,1)S(1)} %copy-done.4, bf16[1024,512]{1,0:T(8,128)(2,1)S(1)} %copy-done.3, bf16[512,512]{0,1:T(8,128)(2,1)S(1)} %fusion.6, bf16[512,512]{0,1:T(8,128)(2,1)S(1)} %copy.23), kind=kOutput, calls=%fused_computation.13 | convolution fusion | flops 542113792 | bytes 3670016 | tf_op jit(solution)/shard_map/dot_general | solution.py:42
  35.5 2.1 %fusion.10 = f32[1024,512]{1,0:T(8,128)} fusion(bf16[512,512]{1,0:T(8,128)(2,1)S(1)} %get-tuple-element.3, bf16[512,512]{0,1:T(8,128)(2,1)S(1)} %fusion.6, bf16[512,512]{0,1:T(8,128)(2,1)S(1)} %copy.23), kind=kOutput, calls=%fused_computation.17 | convolution fusion | flops 538968064 | bytes 3670016 | tf_op jit(solution)/shard_map/dot_general | solution.py:47
  37.6 0.0 reduce-scatter.5.cloned.1.call-start
  37.6 1.3 fusion.8
  39.0 0.0 all-reduce.2.cloned.1.call-start
  39.0 41.6 %reduce-scatter.3.cloned.1.call-done = f32[256,512]{1,0:T(8,128)} async-done(((f32[1024,512]{1,0:T(8,128)}), f32[256,512]{1,0:T(8,128)}) %reduce-scatter.3.cloned.1.call-update) | async-done | bytes 524304 | tf_op jit(solution)/shard_map/reduce_scatter | solution.py:46
  80.7 36.3 %reduce-scatter.5.cloned.1.call-done = f32[8,512]{1,0:T(8,128)} async-done(((f32[64,512]{1,0:T(8,128)}), f32[8,512]{1,0:T(8,128)}) %reduce-scatter.5.cloned.1.call-update) | async-done | bytes 16400 | tf_op jit(solution)/shard_map/reduce_scatter | solution.py:58
  117.0 19.9 %psum.15 = f32[8,512]{1,0:T(8,128)} all-reduce(f32[8,512]{1,0:T(8,128)} %reduce-scatter.5.cloned.1.call-done), channel_id=1, replica_groups=mesh['region'=8,'dom'=4] {'dom'}, use_global_device_ids=true, to_apply=%region_6.7 | all-reduce | flops 4096 | bytes 32768 | tf_op jit(solution)/shard_map/psum | solution.py:64
  136.9 38.0 %all-reduce.2.cloned.1.call-done = f32[256,512]{1,0:T(8,128)} async-done(((f32[256,512]{1,0:T(8,128)}), f32[256,512]{1,0:T(8,128)}) %all-reduce.2.cloned.1.call-update) | async-done | bytes 524304 | tf_op jit(solution)/shard_map/psum | solution.py:52
  174.9 1.9 %copy.30 = f32[256,512]{1,0:T(8,128)} copy(f32[256,512]{1,0:T(8,128)} %all-reduce.2.cloned.1.call-done) | data formatting | bytes 1048576
  (16 shorter events, 0.2 us)
Async XLA Ops:
  7.2 20.3 %copy-start = (bf16[512,512]{1,0:T(8,128)(2,1)S(1)}, bf16[512,512]{1,0:T(8,128)(2,1)}, u32[]{:S(2)}) copy-start(bf16[512,512]{1,0:T(8,128)(2,1)} %param.7) | copy-start | bytes 1572868
  7.2 11.0 %copy-start.2 = (bf16[8,512]{1,0:T(8,128)(2,1)S(1)}, bf16[8,512]{1,0:T(8,128)(2,1)}, u32[]{:S(2)}) copy-start(bf16[8,512]{1,0:T(8,128)(2,1)} %param.8) | copy-start | bytes 24580
  7.2 73.4 %reduce-scatter.3.cloned.1.call-start = ((), (), s32[]{:S(2)}) async-start(), calls=%async_computation.2 | async-start | bytes 2621440 | tf_op jit(solution)/shard_map/reduce_scatter | solution.py:46
  8.2 19.3 %collective-permute-start = (bf16[128,512]{1,0:T(8,128)(2,1)S(1)}, bf16[128,512]{1,0:T(8,128)(2,1)S(1)}, u32[]{:S(2)}, u32[]{:S(2)}) collective-permute-start(bf16[128,512]{1,0:T(8,128)(2,1)S(1)} %slice.18), channel_id=1, source_target_pairs={{0,1},{1,2},{2,3},{4,5},{5,6},{6,7},{8,9},{9,10},{10,11},{12,13},{... | collective-permute-start | bytes 393224 | tf_op jit(solution)/shard_map/ppermute | solution.py:10
  27.6 2.0 %copy-start.1 = (s32[16,128,128]{2,1,0:T(8,128)S(1)}, s32[16,128,128]{2,1,0:T(8,128)}, u32[]{:S(2)}) copy-start(s32[16,128,128]{2,1,0:T(8,128)} %param.11) | copy-start | bytes 3145732
  32.2 1.2 copy-start.3
  32.2 1.3 copy-start.4
  37.6 79.4 %reduce-scatter.5.cloned.1.call-start = ((), (), s32[]{:S(2)}) async-start(), calls=%async_computation.4 | async-start | bytes 147456 | tf_op jit(solution)/shard_map/reduce_scatter | solution.py:58
  39.0 135.9 %all-reduce.2.cloned.1.call-start = ((), (), s32[]{:S(2)}) async-start(), calls=%async_computation.3 | async-start | bytes 1048576 | tf_op jit(solution)/shard_map/psum | solution.py:52
Sparse Core Ops, SparseCore 0:
  37.7 42.8 reduce-scatter.2
  84.2 32.7 reduce-scatter.4
  120.1 54.7 all-reduce.1
where the time goes:
time: 184 us; the launch traced here: 183 us
  waiting for transfers between devices  116 us (63%)
  blocking collectives  29.2 us (16%)
  between operations  13.9 us (8%)
  matrix products  8.9 us (5%)
  local copies, waits for them, and re-layouts  7.35 us (4%)
  starting transfers between devices  5.08 us (3%)
  other arithmetic  2.97 us (2%)
    reduce_scatter x1, waiting for transfers between devices, on_device(): lax.psum_scatter(lax.dot_general(inputs, dz, (((0,), (0,)), ((), ())), pr...  41.6 us
    psum x1, waiting for transfers between devices, on_device(): weight_grad = lax.psum(partial_w, 'region')  38 us
    reduce_scatter x1, waiting for transfers between devices, on_device(): lax.psum_scatter(lax.dot_general(block, sgrad, (((0,), (0,)), ((), ())),...  36.3 us
    psum x1, blocking collectives, on_device(): hub_grad = lax.psum(region_sum, 'dom')  19.9 us
    all_gather x1, blocking collectives, on_device(): lax.all_gather(hub_feats, 'region', axis=0, tiled=True)  9.26 us
    ppermute x1, starting transfers between devices, shifted(): lax.ppermute(value, axis, [(source, source + steps) for source in range(i...  4.96 us
  transfers between devices with their start and end apart: 4, of which 3 were waited for; matrix products, arithmetic and copies ran while one was open for 3% of the time, Pallas kernels for 0%

commit v1 on v0

--- a/solution.py
+++ b/solution.py
@@ -49,7 +49,7 @@
         scatter_dimension=0,
         tiled=True,
     )
-    weight_grad = lax.psum(partial_w, "region")
+    weight_grad = lax.all_gather(partial_w, "region").sum(axis=0)
     dagg = lax.dot_general(
         dz, w_stack[width:], (((1,), (1,)), ((), ())), preferred_element_type=jnp.float32
     )

time: 184 us -> 166 us (0.902)
  waiting for transfers between devices: 116 us -> 96.5 us
  other arithmetic: 2.97 us -> 6.45 us
  local copies, waits for them, and re-layouts: 7.35 us -> 5.48 us
    psum x1 -> x0, waiting for transfers between devices: 38 us -> none  [on_device(): weight_grad = lax.psum(partial_w, 'region')]
    all_gather x0 -> x1, waiting for transfers between devices: none -> 18.6 us  [on_device(): weight_grad = lax.all_gather(partial_w, 'region').sum(axis=0)]
    reduce_sum x0 -> x1, other arithmetic: none -> 3.49 us  [on_device(): weight_grad = lax.all_gather(partial_w, 'region').sum(axis=0)]
    unnamed x12 -> x11, local copies, waits for them, and re-layouts: 3.5 us -> 1.63 us
  transfers between devices with their start and end apart: 4 -> 4, of which waited for: 3 -> 3; matrix products, arithmetic and copies ran while one was open for 3% -> 4% of each run, Pallas kernels for 0% -> 0%
where the time goes in v1:
time: 166 us
  waiting for transfers between devices  96.5 us (58%)
  blocking collectives  29.2 us (18%)
  between operations  13.9 us (8%)
  matrix products  8.9 us (5%)
  other arithmetic  6.45 us (4%)
  local copies, waits for them, and re-layouts  5.48 us (3%)
  starting transfers between devices  5.08 us (3%)
    reduce_scatter x1, waiting for transfers between devices, on_device(): lax.psum_scatter(lax.dot_general(inputs, dz, (((0,), (0,)), ((), ())), pr...  41.6 us
    reduce_scatter x1, waiting for transfers between devices, on_device(): lax.psum_scatter(lax.dot_general(block, sgrad, (((0,), (0,)), ((), ())),...  36.3 us
    psum x1, blocking collectives, on_device(): hub_grad = lax.psum(region_sum, 'dom')  19.9 us
    all_gather x1, waiting for transfers between devices, on_device(): weight_grad = lax.all_gather(partial_w, 'region').sum(axis=0)  18.6 us
    all_gather x1, blocking collectives, on_device(): lax.all_gather(hub_feats, 'region', axis=0, tiled=True)  9.26 us
    ppermute x1, starting transfers between devices, shifted(): lax.ppermute(value, axis, [(source, source + steps) for source in range(i...  4.96 us
    reduce_sum x1, other arithmetic, on_device(): weight_grad = lax.all_gather(partial_w, 'region').sum(axis=0)  3.49 us
  transfers between devices with their start and end apart: 4, of which 3 were waited for; matrix products, arithmetic and copies ran while one was open for 4% of the time, Pallas kernels for 0%

profile of v1, /device:TPU:0, one launch (start us, length us, event | category | flops | bytes accessed | tf_op | source)
XLA Modules:
  0.0 165.5 jit_solution(13485696315172568815)
XLA Ops:
  7.2 0.0 reduce-scatter.3.cloned.1.call-start
  7.2 1.0 slice.18
  8.2 5.0 %collective-permute-start = (bf16[128,512]{1,0:T(8,128)(2,1)S(1)}, bf16[128,512]{1,0:T(8,128)(2,1)S(1)}, u32[]{:S(2)}, u32[]{:S(2)}) collective-permute-start(bf16[128,512]{1,0:T(8,128)(2,1)S(1)} %slice.18), channel_id=1, source_target_pairs={{0,1},{1,2},{2,3},{4,5},{5,6},{6,7},{8,9},{9,10},{10,11},{12,13},{... | collective-permute-start | bytes 393224 | tf_op jit(solution)/shard_map/ppermute | solution.py:10
  13.2 0.7 compare_and_fusion
  13.8 1.6 reduce_sum.35
  15.4 0.9 fusion.19
  16.3 0.7 compare_select_fusion
  17.0 1.3 copy.23
  18.2 9.3 %all_gather.9 = bf16[64,512]{1,0:T(8,128)(2,1)S(1)} all-gather(bf16[8,512]{1,0:T(8,128)(2,1)S(1)} %copy-done.2), channel_id=1, replica_groups=mesh['region'=8,'dom'=4] {'region'}, dimensions={0}, use_global_device_ids=true | all-gather | bytes 73728 | tf_op jit(solution)/shard_map/all_gather | solution.py:37
  27.6 2.0 %gather_fusion = bf16[16,128,512]{2,1,0:T(8,128)(2,1)} fusion(bf16[5,128,512]{2,1,0:T(8,128)(2,1)S(1)} %bitcast.24, s32[1024]{0:T(1024)S(1)} %pad_clamp_fusion), kind=kCustom, calls=%fused_computation | custom fusion | bytes 4194368 | tf_op jit(solution)/shard_map/jit(_take)/gather | solution.py:23
  29.6 2.6 %bitcast_reduce_fusion = f32[4,128,512]{1,2,0:T(8,128)S(1)} fusion(bf16[16,128,512]{2,1,0:T(8,128)(2,1)} %gather_fusion, pred[16]{0:T(512)(128)(4,1)S(1)} %compare_and_fusion, s32[16,128,128]{2,1,0:T(8,128)S(1)} %copy-done.1), kind=kOutput, calls=%fused_computation.1 | convolution fusion | flops 270532608 | bytes 4194320 | tf_op jit(solution)/shard_map/tij,tjd->tid/dot_general | solution.py:25
  32.2 1.0 fusion.6
  33.2 0.2 copy-done.3
  33.5 0.1 copy-done.4
  33.6 1.9 %multiply_convert_fusion = (bf16[512,512]{1,0:T(8,128)(2,1)S(1)}, bf16[512,512]{1,0:T(8,128)(2,1)}) fusion(bf16[512,512]{1,0:T(8,128)(2,1)S(1)} %copy-done.4, bf16[1024,512]{1,0:T(8,128)(2,1)S(1)} %copy-done.3, bf16[512,512]{0,1:T(8,128)(2,1)S(1)} %fusion.6, bf16[512,512]{0,1:T(8,128)(2,1)S(1)} %copy.23), kind=kOutput, calls=%fused_computation.13 | convolution fusion | flops 542113792 | bytes 3670016 | tf_op jit(solution)/shard_map/dot_general | solution.py:42
  35.5 2.1 %fusion.10 = f32[1024,512]{1,0:T(8,128)} fusion(bf16[512,512]{1,0:T(8,128)(2,1)S(1)} %get-tuple-element.3, bf16[512,512]{0,1:T(8,128)(2,1)S(1)} %fusion.6, bf16[512,512]{0,1:T(8,128)(2,1)S(1)} %copy.23), kind=kOutput, calls=%fused_computation.17 | convolution fusion | flops 538968064 | bytes 3670016 | tf_op jit(solution)/shard_map/dot_general | solution.py:47
  37.6 0.0 reduce-scatter.5.cloned.1.call-start
  37.6 1.3 fusion.8
  39.0 0.0 all-gather.3.cloned.1.call-start
  39.0 41.6 %reduce-scatter.3.cloned.1.call-done = f32[256,512]{1,0:T(8,128)} async-done(((f32[1024,512]{1,0:T(8,128)}), f32[256,512]{1,0:T(8,128)}) %reduce-scatter.3.cloned.1.call-update) | async-done | bytes 524304 | tf_op jit(solution)/shard_map/reduce_scatter | solution.py:46
  80.7 36.3 %reduce-scatter.5.cloned.1.call-done = f32[8,512]{1,0:T(8,128)} async-done(((f32[64,512]{1,0:T(8,128)}), f32[8,512]{1,0:T(8,128)}) %reduce-scatter.5.cloned.1.call-update) | async-done | bytes 16400 | tf_op jit(solution)/shard_map/reduce_scatter | solution.py:58
  117.0 19.9 %psum.7 = f32[8,512]{1,0:T(8,128)} all-reduce(f32[8,512]{1,0:T(8,128)} %reduce-scatter.5.cloned.1.call-done), channel_id=1, replica_groups=mesh['region'=8,'dom'=4] {'dom'}, use_global_device_ids=true, to_apply=%region_6.7 | all-reduce | flops 4096 | bytes 32768 | tf_op jit(solution)/shard_map/psum | solution.py:64
  136.9 18.6 %all-gather.3.cloned.1.call-done = f32[2048,512]{1,0:T(8,128)} async-done(((f32[256,512]{1,0:T(8,128)}), f32[2048,512]{1,0:T(8,128)}) %all-gather.3.cloned.1.call-update) | async-done | bytes 4194320 | tf_op jit(solution)/shard_map/all_gather | solution.py:52
  155.5 3.5 %reduce_sum.38 = f32[256,512]{1,0:T(8,128)} reduce(f32[8,256,512]{2,1,0:T(8,128)} %bitcast.25, f32[]{:T(128)} %constant.22.clone.1), dimensions={0}, to_apply=%region_4.5 | reduce | flops 917504 | bytes 4718596 | tf_op jit(solution)/shard_map/reduce_sum | solution.py:52
  (16 shorter events, 0.2 us)
Async XLA Ops:
  7.2 20.3 %copy-start = (bf16[512,512]{1,0:T(8,128)(2,1)S(1)}, bf16[512,512]{1,0:T(8,128)(2,1)}, u32[]{:S(2)}) copy-start(bf16[512,512]{1,0:T(8,128)(2,1)} %param.7) | copy-start | bytes 1572868
  7.2 11.0 %copy-start.2 = (bf16[8,512]{1,0:T(8,128)(2,1)S(1)}, bf16[8,512]{1,0:T(8,128)(2,1)}, u32[]{:S(2)}) copy-start(bf16[8,512]{1,0:T(8,128)(2,1)} %param.8) | copy-start | bytes 24580
  7.2 73.4 %reduce-scatter.3.cloned.1.call-start = ((), (), s32[]{:S(2)}) async-start(), calls=%async_computation.2 | async-start | bytes 2621440 | tf_op jit(solution)/shard_map/reduce_scatter | solution.py:46
  8.2 19.3 %collective-permute-start = (bf16[128,512]{1,0:T(8,128)(2,1)S(1)}, bf16[128,512]{1,0:T(8,128)(2,1)S(1)}, u32[]{:S(2)}, u32[]{:S(2)}) collective-permute-start(bf16[128,512]{1,0:T(8,128)(2,1)S(1)} %slice.18), channel_id=1, source_target_pairs={{0,1},{1,2},{2,3},{4,5},{5,6},{6,7},{8,9},{9,10},{10,11},{12,13},{... | collective-permute-start | bytes 393224 | tf_op jit(solution)/shard_map/ppermute | solution.py:10
  27.6 2.0 %copy-start.1 = (s32[16,128,128]{2,1,0:T(8,128)S(1)}, s32[16,128,128]{2,1,0:T(8,128)}, u32[]{:S(2)}) copy-start(s32[16,128,128]{2,1,0:T(8,128)} %param.11) | copy-start | bytes 3145732
  32.2 1.2 copy-start.3
  32.2 1.3 copy-start.4
  37.6 79.4 %reduce-scatter.5.cloned.1.call-start = ((), (), s32[]{:S(2)}) async-start(), calls=%async_computation.3 | async-start | bytes 147456 | tf_op jit(solution)/shard_map/reduce_scatter | solution.py:58
  39.0 116.5 %all-gather.3.cloned.1.call-start = ((), (), s32[]{:S(2)}) async-start(), calls=%async_computation.4 | async-start | bytes 4718592 | tf_op jit(solution)/shard_map/all_gather | solution.py:52
Sparse Core Ops, SparseCore 0:
  37.7 42.8 reduce-scatter.2
  84.2 32.7 reduce-scatter.4
  118.9 36.5 all-gather.2
